TPU v7x, 32 devices: a whole 2x2x4 slice. The times are simulated.
32 devices in a mesh: tile: 8 (over y, x, core), slab: 4 (over z).
Axes of the slice: x: 2, y: 2, z: 4, core: 2. Of those that a mesh axis runs over, the one named last changes fastest.
Arguments:
- estimate: float32 [64, 128, 512], P('slab', 'tile'), may hold values from 0.5 to 2
- observed: float32 [64, 128, 512], P('slab', 'tile'), may hold values from 0.25 to 4
- kernel_rows: float32 [31], replicated, may hold values from 0.001 to 1
- kernel_columns: float32 [31], replicated, may hold values from 0.001 to 1
- kernel_planes: float32 [31], replicated, may hold values from 0.001 to 1
Outputs:
- new_estimate: float32 [64, 128, 512], P('slab', 'tile')
- pyramid_level: float32 [64, 64, 256], P('slab', 'tile')
All inputs are finite; a program needn't handle non-finite values.
Results may differ from a plain program's by a relative error of at most 0.00005.
Values sent between devices are 32-bit elements; how exact they have to be, the bound alone decides.
No kernel may reach another device: no remote copies, remote signals or barrier semaphores. Data moves between devices by JAX's collectives and lax.ppermute only.
A program may use at most 64 MiB of HBM per device.

v0:
```python
import jax
import jax.numpy as jnp
from jax import lax
from jax.sharding import PartitionSpec as P

PRECISE = lax.Precision.HIGHEST


def extended(shard, sides, width):
    for axis, dim in sides:
        devices, length = (lax.axis_size(axis), shard.shape[dim])
        up = [(i, (i + 1) % devices) for i in range(devices - 1)]
        down = [(j, i) for i, j in up]
        last = lax.slice_in_dim(shard, length - width, length, axis=dim)
        initial = lax.slice_in_dim(shard, 0, width, axis=dim)
        before = lax.ppermute(last, axis, up)
        after = lax.ppermute(initial, axis, down)
        shard = jnp.concatenate([before, shard, after], axis=dim)
    return shard


def banded(kernel, row_count, col_count, orient, anchor):
    tap_count = kernel.shape[0]
    offset_index = (
        orient
        * (
            lax.broadcasted_iota(jnp.int32, (row_count, col_count), 0)
            - lax.broadcasted_iota(jnp.int32, (row_count, col_count), 1)
        )
        + anchor
    )
    inside = (offset_index >= 0) & (offset_index < tap_count)
    values = jnp.take(kernel, jnp.clip(offset_index, 0, tap_count - 1))
    return jnp.where(inside, values, jnp.zeros_like(values))


def pyramid_matrix(row_count, col_count, anchor):
    offset_index = (
        lax.broadcasted_iota(jnp.int32, (row_count, col_count), 0)
        - 2 * lax.broadcasted_iota(jnp.int32, (row_count, col_count), 1)
        + anchor
    )
    outer = (offset_index == 0) | (offset_index == 3)
    middle = (offset_index == 1) | (offset_index == 2)
    return jnp.where(
        outer, jnp.float32(0.125), jnp.where(middle, jnp.float32(0.375), jnp.float32(0.0))
    )


def across_depth(volume, matrix):
    return jnp.einsum("pxy,pq->qxy", volume, matrix, precision=PRECISE)


def across_rows(volume, matrix):
    return jnp.einsum("zpy,pq->zqy", volume, matrix, precision=PRECISE)


def across_columns(volume, matrix):
    return jnp.dot(volume, matrix, precision=PRECISE)


def shards(estimate, observed, kernel_rows, kernel_columns, kernel_planes):
    plane_count, row_count, col_count = estimate.shape
    reach_cells = (kernel_rows.shape[0] - 1) // 2
    groups = lax.axis_size("slab")
    planes_all = plane_count * groups
    padded = extended(estimate, (("tile", 1),), reach_cells)
    partial_value = across_rows(
        padded, banded(kernel_rows, row_count + 2 * reach_cells, row_count, 1, 0)
    )
    partial_value = across_columns(
        partial_value, banded(kernel_columns, col_count, col_count, 1, reach_cells)
    )
    forward_depth = banded(kernel_planes, planes_all, planes_all, 1, reach_cells)
    backward_depth = banded(kernel_planes, planes_all, planes_all, -1, reach_cells)
    turned = across_depth(
        lax.all_to_all(partial_value, "slab", split_axis=2, concat_axis=0, tiled=True),
        forward_depth,
    )
    blurred = lax.all_to_all(turned, "slab", split_axis=0, concat_axis=2, tiled=True)
    quotient = observed / blurred
    turned_back = across_depth(
        lax.all_to_all(quotient, "slab", split_axis=2, concat_axis=0, tiled=True), backward_depth
    )
    back_field = lax.all_to_all(turned_back, "slab", split_axis=0, concat_axis=2, tiled=True)
    spread = across_columns(
        back_field, banded(kernel_columns, col_count, col_count, -1, reach_cells)
    )
    padded_spread = extended(spread, (("tile", 1),), reach_cells)
    correction = across_rows(
        padded_spread,
        banded(kernel_rows, row_count + 2 * reach_cells, row_count, -1, 2 * reach_cells),
    )
    new_estimate = estimate * correction
    halved = across_columns(new_estimate, pyramid_matrix(col_count, col_count // 2, 1))
    padded_halved = extended(halved, (("tile", 1),), 1)
    pyramid_level = across_rows(padded_halved, pyramid_matrix(row_count + 2, row_count // 2, 0))
    return (new_estimate, pyramid_level)


def solution(mesh):
    in_specs = (P("slab", "tile", None), P("slab", "tile", None), P(), P(), P())
    out_specs = (P("slab", "tile", None), P("slab", "tile", None))
    return jax.shard_map(shards, mesh=mesh, in_specs=in_specs, out_specs=out_specs, check_vma=False)
```

profile of v0, /device:TPU:1, one launch (start us, length us, event | category | flops | bytes accessed | tf_op | source)
XLA Modules:
  0.0 230.6 jit_solution(3255726964246776414)
XLA Ops:
  0.7 1.3 fusion.571
  2.0 4.5 %collective-permute-start = (f32[16,15,512]{2,1,0:T(8,128)S(1)}, f32[16,15,512]{2,1,0:T(8,128)S(1)}, u32[]{:S(2)}, u32[]{:S(2)}) collective-permute-start(f32[16,15,512]{2,1,0:T(8,128)S(1)} %get-tuple-element.7), channel_id=1, source_target_pairs={{0,4},{4,8},{8,12},{12,16},{16,20},{20,24},{24,28},{1,5},{5,9},{9,... | collective-permute-start | bytes 1474568 | tf_op jit(solution)/shard_map/ppermute | solution.py:16
  6.5 1.9 collective-permute-start.1
  8.5 0.1 reshape.155
  8.6 4.8 %gather_fusion.3 = f32[736]{0:T(1024)S(1)} fusion(f32[31]{0:T(128)S(1)} %copy-done.1, s32[1024]{0:T(1024)S(1)} %pad_clamp_fusion), kind=kCustom, calls=%fused_computation.2.clone | custom fusion | bytes 8832 | tf_op jit(solution)/shard_map/jit(_take)/gather | solution.py:33
  13.5 0.7 fusion.574
  14.2 0.7 fusion.573
  14.9 5.0 %collective-permute-done.1 = f32[16,15,512]{2,1,0:T(8,128)S(1)} collective-permute-done((f32[16,15,512]{2,1,0:T(8,128)S(1)}, f32[16,15,512]{2,1,0:T(8,128)S(1)}, u32[]{:S(2)}, u32[]{:S(2)}) %collective-permute-start.1) | collective-permute-done | bytes 491552 | tf_op jit(solution)/shard_map/ppermute | solution.py:17
  19.9 1.0 fusion.15
  20.9 23.0 %fusion.23 = f32[16,16,512]{2,1,0:T(8,128)S(1)} fusion(f32[16,16,512]{2,1,0:T(8,128)S(1)} %fusion.15, f32[]{:T(128)} %bitcast.35, f32[]{:T(128)} %bitcast.34, f32[]{:T(128)} %bitcast.33, f32[]{:T(128)} %bitcast.32, f32[]{:T(128)} %bitcast.31, f32[]{:T(128)} %bitcast.30, f32[]{:T(128)} %bitcast.29, f32[]{:T(128)} %bitcast.28, f32[]{:T(128)} %bitcast.27, ...), kind=kOutput, calls=%fused_computation.25 | convolution fusion | flops 824705024 | bytes 1048700 | tf_op jit(solution)/shard_map/dot_general | solution.py:59
  43.9 3.6 %copy.19 = f32[16,16,512]{1,0,2:T(8,128)} copy(f32[16,16,512]{2,1,0:T(8,128)S(1)} %fusion.23) | data formatting | bytes 1048576 | tf_op jit(solution)/shard_map/dot_general | solution.py:59
  47.5 4.6 %reshape.229 = f32[4,1,32768]{2,1,0:T(1,128)} reshape(f32[512,16,16]{2,1,0:T(8,128)} %bitcast.121) | data formatting | bytes 1048576
  52.1 4.6 %all-to-all-start = ((f32[4,1,32768]{2,1,0:T(1,128)}), f32[4,1,32768]{2,1,0:T(1,128)S(1)}, u32[]{:S(2)}, u32[]{:S(2)}) async-start(f32[4,1,32768]{2,1,0:T(1,128)} %reshape.229), calls=%async_computation | async-start | bytes 1048576 | tf_op jit(solution)/shard_map/all_to_all | solution.py:77
  56.8 24.7 %gather_fusion.2 = f32[4096]{0:T(1024)S(1)} fusion(f32[31]{0:T(128)S(1)} %copy-done, s32[4096]{0:T(1024)S(1)} %broadcast_clamp_fusion), kind=kCustom, calls=%fused_computation.3.clone | custom fusion | bytes 49152 | tf_op jit(solution)/shard_map/jit(_take)/gather | solution.py:33
  81.6 0.5 broadcast.948
  82.1 2.1 reduce
  84.2 3.4 %reshape.230 = f32[512,16,16]{2,1,0:T(8,128)} reshape(f32[4,32768]{1,0:T(4,128)S(1)} %reduce) | data formatting | bytes 1048576
  87.7 3.3 %copy.20 = f32[16,16,4,128]{3,0,2,1:T(8,128)S(1)} copy(f32[16,16,4,128]{1,0,3,2:T(8,128)} %bitcast.122) | data formatting | bytes 1048576 | tf_op jit(solution)/shard_map/all_to_all | solution.py:77
  91.0 0.6 fusion.379
  91.7 1.1 copy.22
  92.8 4.5 %all-to-all-start.1 = ((f32[64,16,128]{2,1,0:T(8,128)}), f32[64,16,128]{2,1,0:T(8,128)S(1)}, u32[]{:S(2)}, u32[]{:S(2)}) async-start(f32[64,16,128]{2,1,0:T(8,128)} %copy.22), calls=%async_computation.1 | async-start | bytes 1048576 | tf_op jit(solution)/shard_map/all_to_all | solution.py:80
  97.3 3.7 %copy.24 = f32[16,16,512]{1,0,2:T(8,128)} copy(f32[16,16,512]{2,1,0:T(8,128)S(1)} %copy-done.3) | data formatting | bytes 1048576 | tf_op args[1]
  100.9 5.6 %all-to-all-done.1 = f32[64,16,128]{2,1,0:T(8,128)S(1)} async-done(((f32[64,16,128]{2,1,0:T(8,128)}), f32[64,16,128]{2,1,0:T(8,128)S(1)}, u32[]{:S(2)}, u32[]{:S(2)}) %all-to-all-start.1) | async-done | bytes 524320 | tf_op jit(solution)/shard_map/all_to_all | solution.py:80
  106.5 2.8 %copy.23 = f32[16,16,4,128]{1,0,3,2:T(8,128)} copy(f32[16,16,4,128]{3,1,0,2:T(8,128)S(1)} %bitcast.124) | data formatting | bytes 1048576 | tf_op jit(solution)/shard_map/all_to_all | solution.py:80
  109.3 6.0 %bitcast_divide_fusion = f32[16,16,512]{1,0,2:T(8,128)} fusion(f32[16,16,512]{1,0,2:T(8,128)} %copy.24, f32[16,16,4,128]{1,0,3,2:T(8,128)} %copy.23), kind=kLoop, calls=%fused_computation.4 | loop fusion | flops 131072 | bytes 1572864 | tf_op jit(solution)/shard_map/div | solution.py:81
  115.3 4.6 %reshape.231 = f32[4,1,32768]{2,1,0:T(1,128)} reshape(f32[512,16,16]{2,1,0:T(8,128)} %bitcast.120) | data formatting | bytes 1048576
  119.9 3.5 %all-to-all-start.2 = ((f32[4,1,32768]{2,1,0:T(1,128)}), f32[4,1,32768]{2,1,0:T(1,128)S(1)}, u32[]{:S(2)}, u32[]{:S(2)}) async-start(f32[4,1,32768]{2,1,0:T(1,128)} %reshape.231), calls=%async_computation.2 | async-start | bytes 1048576 | tf_op jit(solution)/shard_map/all_to_all | solution.py:83
  123.5 24.7 %gather_fusion.1 = f32[4096]{0:T(1024)S(1)} fusion(f32[31]{0:T(128)S(1)} %copy-done, s32[4096]{0:T(1024)S(1)} %broadcast_clamp_fusion.1), kind=kCustom, calls=%fused_computation.1.clone | custom fusion | bytes 49152 | tf_op jit(solution)/shard_map/jit(_take)/gather | solution.py:33
  148.3 2.1 reduce.1
  150.4 3.4 %reshape.232 = f32[512,16,16]{2,1,0:T(8,128)} reshape(f32[4,32768]{1,0:T(4,128)S(1)} %reduce.1) | data formatting | bytes 1048576
  153.8 3.3 %copy.25 = f32[16,16,4,128]{3,0,2,1:T(8,128)S(1)} copy(f32[16,16,4,128]{1,0,3,2:T(8,128)} %bitcast.123) | data formatting | bytes 1048576 | tf_op jit(solution)/shard_map/all_to_all | solution.py:83
  157.2 0.6 fusion.381
  157.8 0.3 copy.27
  158.1 15.2 %all_to_all.72 = f32[64,16,128]{2,1,0:T(8,128)S(1)} all-to-all(f32[64,16,128]{2,1,0:T(8,128)S(1)} %copy.27), channel_id=1, replica_groups=mesh['tile'=8,'slab'=4] {'slab'}, dimensions={0} | all-to-all | bytes 1048576 | tf_op jit(solution)/shard_map/all_to_all | solution.py:85
  173.4 0.3 copy.39
  173.7 0.2 all_to_all.67
  174.0 22.9 %fusion.21 = f32[16,16,512]{2,1,0:T(8,128)S(1)} fusion(f32[16,16,512]{2,1,0:T(8,128)S(1)} %all_to_all.67, f32[]{:T(128)} %bitcast.35, f32[]{:T(128)} %bitcast.34, f32[]{:T(128)} %bitcast.33, f32[]{:T(128)} %bitcast.32, f32[]{:T(128)} %bitcast.31, f32[]{:T(128)} %bitcast.30, f32[]{:T(128)} %bitcast.29, f32[]{:T(128)} %bitcast.28, f32[]{:T(128)} %bitcast.27, ...), kind=kOutput, calls=%fused_computation.23 | convolution fusion | flops 824967168 | bytes 1048700 | tf_op jit(solution)/shard_map/dot_general | solution.py:59
  196.9 0.1 fusion.570
  197.0 13.3 %collective-permute-start.2 = (f32[16,15,512]{2,1,0:T(8,128)S(1)}, f32[16,15,512]{2,1,0:T(8,128)S(1)}, u32[]{:S(2)}, u32[]{:S(2)}) collective-permute-start(f32[16,15,512]{2,1,0:T(8,128)S(1)} %get-tuple-element.4), channel_id=1, source_target_pairs={{0,4},{4,8},{8,12},{12,16},{16,20},{20,24},{24,28},{1,5},{5,9},{9,... | collective-permute-start | bytes 1474568 | tf_op jit(solution)/shard_map/ppermute | solution.py:16
  210.3 2.1 collective-permute-start.3
  212.5 4.8 %gather_fusion = f32[736]{0:T(1024)S(1)} fusion(f32[31]{0:T(128)S(1)} %copy-done.1, s32[1024]{0:T(1024)S(1)} %pad_clamp_fusion.1), kind=kCustom, calls=%fused_computation.clone | custom fusion | bytes 8832 | tf_op jit(solution)/shard_map/jit(_take)/gather | solution.py:33
  217.4 3.4 %collective-permute-done.3 = f32[16,15,512]{2,1,0:T(8,128)S(1)} collective-permute-done((f32[16,15,512]{2,1,0:T(8,128)S(1)}, f32[16,15,512]{2,1,0:T(8,128)S(1)}, u32[]{:S(2)}, u32[]{:S(2)}) %collective-permute-start.3) | collective-permute-done | bytes 491552 | tf_op jit(solution)/shard_map/ppermute | solution.py:17
  220.8 1.0 fusion.18
  221.8 0.7 fusion.223
  222.6 1.9 collective-permute-start.4
  224.5 2.4 %collective-permute-start.5 = (f32[16,1,256]{2,1,0:T(1,128)S(1)}, f32[16,1,256]{2,1,0:T(1,128)S(1)}, u32[]{:S(2)}, u32[]{:S(2)}) collective-permute-start(f32[16,1,256]{2,1,0:T(1,128)S(1)} %get-tuple-element.10), channel_id=1, source_target_pairs={{4,0},{8,4},{12,8},{16,12},{20,16},{24,20},{28,24},{5,1},{9,5},{13... | collective-permute-start | bytes 49160 | tf_op jit(solution)/shard_map/ppermute | solution.py:17
  226.9 2.6 %collective-permute-done.5 = f32[16,1,256]{2,1,0:T(1,128)S(1)} collective-permute-done((f32[16,1,256]{2,1,0:T(1,128)S(1)}, f32[16,1,256]{2,1,0:T(1,128)S(1)}, u32[]{:S(2)}, u32[]{:S(2)}) %collective-permute-start.5) | collective-permute-done | bytes 16416 | tf_op jit(solution)/shard_map/ppermute | solution.py:17
  229.6 1.0 convolution_bitcast_fusion
  (35 shorter events, 0.7 us)
Async XLA Ops:
  0.6 56.2 %copy-start = (f32[31]{0:T(128)S(1)}, f32[31]{0:T(128)}, u32[]{:S(2)}) copy-start(f32[31]{0:T(128)} %param.15) | copy-start | bytes 376
  0.6 7.9 %copy-start.1 = (f32[31]{0:T(128)S(1)}, f32[31]{0:T(128)}, u32[]{:S(2)}) copy-start(f32[31]{0:T(128)} %param.13) | copy-start | bytes 376
  2.0 12.9 %collective-permute-start = (f32[16,15,512]{2,1,0:T(8,128)S(1)}, f32[16,15,512]{2,1,0:T(8,128)S(1)}, u32[]{:S(2)}, u32[]{:S(2)}) collective-permute-start(f32[16,15,512]{2,1,0:T(8,128)S(1)} %get-tuple-element.7), channel_id=1, source_target_pairs={{0,4},{4,8},{8,12},{12,16},{16,20},{20,24},{24,28},{1,5},{5,9},{9,... | collective-permute-start | bytes 1474568 | tf_op jit(solution)/shard_map/ppermute | solution.py:16
  6.5 13.4 %collective-permute-start.1 = (f32[16,15,512]{2,1,0:T(8,128)S(1)}, f32[16,15,512]{2,1,0:T(8,128)S(1)}, u32[]{:S(2)}, u32[]{:S(2)}) collective-permute-start(f32[16,15,512]{2,1,0:T(8,128)S(1)} %get-tuple-element.8), channel_id=1, source_target_pairs={{4,0},{8,4},{12,8},{16,12},{20,16},{24,20},{28,24},{5,1},{9,5},{13... | collective-permute-start | bytes 1474568 | tf_op jit(solution)/shard_map/ppermute | solution.py:17
  8.6 4.9 %copy-start.5 = (f32[31]{0:T(128)S(1)}, f32[31]{0:T(128)}, u32[]{:S(2)}) copy-start(f32[31]{0:T(128)} %param.14) | copy-start | bytes 376
  8.6 11.3 %copy-start.2 = (f32[16,16,512]{2,1,0:T(8,128)S(1)}, f32[16,16,512]{2,1,0:T(8,128)}, u32[]{:S(2)}) copy-start(f32[16,16,512]{2,1,0:T(8,128)} %param.11) | copy-start | bytes 1572868
  52.1 29.5 %all-to-all-start = ((f32[4,1,32768]{2,1,0:T(1,128)}), f32[4,1,32768]{2,1,0:T(1,128)S(1)}, u32[]{:S(2)}, u32[]{:S(2)}) async-start(f32[4,1,32768]{2,1,0:T(1,128)} %reshape.229), calls=%async_computation | async-start | bytes 1048576 | tf_op jit(solution)/shard_map/all_to_all | solution.py:77
  91.0 6.3 %copy-start.3 = (f32[16,16,512]{2,1,0:T(8,128)S(1)}, f32[16,16,512]{2,1,0:T(8,128)}, u32[]{:S(2)}) copy-start(f32[16,16,512]{2,1,0:T(8,128)} %param.12) | copy-start | bytes 1572868
  92.8 13.7 %all-to-all-start.1 = ((f32[64,16,128]{2,1,0:T(8,128)}), f32[64,16,128]{2,1,0:T(8,128)S(1)}, u32[]{:S(2)}, u32[]{:S(2)}) async-start(f32[64,16,128]{2,1,0:T(8,128)} %copy.22), calls=%async_computation.1 | async-start | bytes 1048576 | tf_op jit(solution)/shard_map/all_to_all | solution.py:80
  119.9 28.4 %all-to-all-start.2 = ((f32[4,1,32768]{2,1,0:T(1,128)}), f32[4,1,32768]{2,1,0:T(1,128)S(1)}, u32[]{:S(2)}, u32[]{:S(2)}) async-start(f32[4,1,32768]{2,1,0:T(1,128)} %reshape.231), calls=%async_computation.2 | async-start | bytes 1048576 | tf_op jit(solution)/shard_map/all_to_all | solution.py:83
  197.0 20.4 %collective-permute-start.2 = (f32[16,15,512]{2,1,0:T(8,128)S(1)}, f32[16,15,512]{2,1,0:T(8,128)S(1)}, u32[]{:S(2)}, u32[]{:S(2)}) collective-permute-start(f32[16,15,512]{2,1,0:T(8,128)S(1)} %get-tuple-element.4), channel_id=1, source_target_pairs={{0,4},{4,8},{8,12},{12,16},{16,20},{20,24},{24,28},{1,5},{5,9},{9,... | collective-permute-start | bytes 1474568 | tf_op jit(solution)/shard_map/ppermute | solution.py:16
  210.3 10.5 %collective-permute-start.3 = (f32[16,15,512]{2,1,0:T(8,128)S(1)}, f32[16,15,512]{2,1,0:T(8,128)S(1)}, u32[]{:S(2)}, u32[]{:S(2)}) collective-permute-start(f32[16,15,512]{2,1,0:T(8,128)S(1)} %get-tuple-element.6), channel_id=1, source_target_pairs={{4,0},{8,4},{12,8},{16,12},{20,16},{24,20},{28,24},{5,1},{9,5},{13... | collective-permute-start | bytes 1474568 | tf_op jit(solution)/shard_map/ppermute | solution.py:17
  221.8 8.8 %copy-start.4 = (f32[16,16,512]{2,1,0:T(8,128)}, f32[16,16,512]{2,1,0:T(8,128)S(1)}, u32[]{:S(2)}) copy-start(f32[16,16,512]{2,1,0:T(8,128)S(1)} %fusion.18) | copy-start | bytes 1572868
  222.6 4.4 %collective-permute-start.4 = (f32[16,1,256]{2,1,0:T(1,128)S(1)}, f32[16,1,256]{2,1,0:T(1,128)S(1)}, u32[]{:S(2)}, u32[]{:S(2)}) collective-permute-start(f32[16,1,256]{2,1,0:T(1,128)S(1)} %get-tuple-element.9), channel_id=1, source_target_pairs={{0,4},{4,8},{8,12},{12,16},{16,20},{20,24},{24,28},{1,5},{5,9},{9,... | collective-permute-start | bytes 49160 | tf_op jit(solution)/shard_map/ppermute | solution.py:16
  224.5 5.1 %collective-permute-start.5 = (f32[16,1,256]{2,1,0:T(1,128)S(1)}, f32[16,1,256]{2,1,0:T(1,128)S(1)}, u32[]{:S(2)}, u32[]{:S(2)}) collective-permute-start(f32[16,1,256]{2,1,0:T(1,128)S(1)} %get-tuple-element.10), channel_id=1, source_target_pairs={{4,0},{8,4},{12,8},{16,12},{20,16},{24,20},{28,24},{5,1},{9,5},{13... | collective-permute-start | bytes 49160 | tf_op jit(solution)/shard_map/ppermute | solution.py:17
where the time goes:
time: 232 us; the launch traced here: 231 us
  local copies, waits for them, and re-layouts  97.8 us (42%)
  matrix products  50.9 us (22%)
  starting transfers between devices  38.8 us (17%)
  waiting for transfers between devices  16.6 us (7%)
  blocking collectives  15.2 us (7%)
  other arithmetic  10.3 us (4%)
    gather x10, local copies, waits for them, and re-layouts, banded(): values = jnp.take(kernel, jnp.clip(offset_index, 0, tap_count - 1))  60.7 us
    dot_general x3, matrix products, across_columns(): return jnp.dot(volume, matrix, precision=PRECISE)  46.6 us
    unnamed x17, local copies, waits for them, and re-layouts  19.8 us
    ppermute x3, starting transfers between devices, extended(): before = lax.ppermute(last, axis, up)  19.7 us
    all_to_all x1, blocking collectives, shards(): lax.all_to_all(turned_back, 'slab', split_axis=0, concat_axis=2, tiled=True)  15.2 us
    ppermute x3, waiting for transfers between devices, extended(): after = lax.ppermute(initial, axis, down)  11 us
    ppermute x3, starting transfers between devices, extended(): after = lax.ppermute(initial, axis, down)  6.46 us
    div x1, other arithmetic, shards(): quotient = observed / blurred  5.99 us
  transfers between devices with their start and end apart: 9, of which 4 were waited for; matrix products, arithmetic and copies ran while one was open for 28% of the time, Pallas kernels for 0%

commit v1 on v0

--- a/solution.py
+++ b/solution.py
@@ -4,6 +4,25 @@
 from jax.sharding import PartitionSpec as P
 
 PRECISE = lax.Precision.HIGHEST
+
+
+def detail_packet_now(inner_x):
+    current_value = lax.axis_size("slab")
+    current_arr = lax.axis_index("slab")
+    arr_out, kept_arr = (current_value, current_arr)
+    passed = inner_x.shape[2] // arr_out
+    big = jnp.roll(inner_x, -kept_arr * passed, 2)
+    opened = lax.slice_in_dim(big, 0, passed, axis=2)
+    shelf = [opened]
+    for tick in range(1, arr_out):
+        mixed_arr = lax.slice_in_dim(big, tick * passed, (tick + 1) * passed, axis=2)
+        small = lax.ppermute(
+            mixed_arr, "slab", perm=[(b, (b + tick) % arr_out) for b in range(arr_out)]
+        )
+        shelf.append(small)
+    built = jnp.concatenate(shelf[::-1], 0)
+    w_next = jnp.roll(built, (kept_arr + 1) * shelf[0].shape[0], 0)
+    return w_next
 
 
 def extended(shard, sides, width):
@@ -73,10 +92,7 @@
     )
     forward_depth = banded(kernel_planes, planes_all, planes_all, 1, reach_cells)
     backward_depth = banded(kernel_planes, planes_all, planes_all, -1, reach_cells)
-    turned = across_depth(
-        lax.all_to_all(partial_value, "slab", split_axis=2, concat_axis=0, tiled=True),
-        forward_depth,
-    )
+    turned = across_depth(detail_packet_now(partial_value), forward_depth)
     blurred = lax.all_to_all(turned, "slab", split_axis=0, concat_axis=2, tiled=True)
     quotient = observed / blurred
     turned_back = across_depth(

time: 232 us -> 218 us (0.940)
  local copies, waits for them, and re-layouts: 97.8 us -> 83 us
  waiting for transfers between devices: 16.6 us -> 22.5 us
  starting transfers between devices: 38.8 us -> 33.4 us
  blocking collectives: 15.2 us -> 18 us
    unnamed x17 -> x22, local copies, waits for them, and re-layouts: 19.8 us -> 11.8 us
    ppermute x0 -> x3, waiting for transfers between devices: none -> 5.15 us  [detail_packet_now(): lax.ppermute(mixed_arr, 'slab', perm=[(b, (b + tick) % arr_out) for b in...]
    all_to_all x1 -> x0, starting transfers between devices: 4.59 us -> none  [shards(): lax.all_to_all(partial_value, 'slab', split_axis=2, concat_axis=0, tiled=...]
    all_to_all x2 -> x0, local copies, waits for them, and re-layouts: 3.84 us -> none  [shards(): lax.all_to_all(partial_value, 'slab', split_axis=2, concat_axis=0, tiled=...]
    ppermute x0 -> x3, starting transfers between devices: none -> 3.81 us  [detail_packet_now(): lax.ppermute(mixed_arr, 'slab', perm=[(b, (b + tick) % arr_out) for b in...]
    dot_general x1 -> x0, local copies, waits for them, and re-layouts: 3.64 us -> none  [across_columns(): return jnp.dot(volume, matrix, precision=PRECISE)]
    ppermute x3, starting transfers between devices: 19.7 us -> 16.2 us  [extended(): before = lax.ppermute(last, axis, up)]
    all_to_all x1, blocking collectives: 15.2 us -> 18 us  [shards(): lax.all_to_all(turned_back, 'slab', split_axis=0, concat_axis=2, tiled=True)]
  transfers between devices with their start and end apart: 9 -> 11, of which waited for: 4 -> 5; matrix products, arithmetic and copies ran while one was open for 28% -> 30% of each run, Pallas kernels for 0% -> 0%
where the time goes in v1:
time: 218 us; the launch traced here: 217 us
  local copies, waits for them, and re-layouts  83 us (38%)
  matrix products  51.1 us (23%)
  starting transfers between devices  33.4 us (15%)
  waiting for transfers between devices  22.5 us (10%)
  blocking collectives  18 us (8%)
  other arithmetic  8.39 us (4%)
    gather x10, local copies, waits for them, and re-layouts, banded(): values = jnp.take(kernel, jnp.clip(offset_index, 0, tap_count - 1))  60.7 us
    dot_general x3, matrix products, across_columns(): return jnp.dot(volume, matrix, precision=PRECISE)  46.7 us
    all_to_all x1, blocking collectives, shards(): lax.all_to_all(turned_back, 'slab', split_axis=0, concat_axis=2, tiled=True)  18 us
    ppermute x3, starting transfers between devices, extended(): before = lax.ppermute(last, axis, up)  16.2 us
    unnamed x22, local copies, waits for them, and re-layouts  11.8 us
    ppermute x3, waiting for transfers between devices, extended(): after = lax.ppermute(initial, axis, down)  11 us
    all_to_all x1, waiting for transfers between devices, shards(): lax.all_to_all(turned, 'slab', split_axis=0, concat_axis=2, tiled=True)  6.38 us
    ppermute x3, starting transfers between devices, extended(): after = lax.ppermute(initial, axis, down)  6.24 us
  transfers between devices with their start and end apart: 11, of which 5 were waited for; matrix products, arithmetic and copies ran while one was open for 30% of the time, Pallas kernels for 0%

profile of v1, /device:TPU:1, one launch (start us, length us, event | category | flops | bytes accessed | tf_op | source)
XLA Modules:
  0.0 217.4 jit_solution(7360512395262926035)
XLA Ops:
  0.7 1.3 fusion.574
  2.0 4.5 %collective-permute-start = (f32[16,15,512]{2,1,0:T(8,128)S(1)}, f32[16,15,512]{2,1,0:T(8,128)S(1)}, u32[]{:S(2)}, u32[]{:S(2)}) collective-permute-start(f32[16,15,512]{2,1,0:T(8,128)S(1)} %get-tuple-element.10), channel_id=1, source_target_pairs={{0,4},{4,8},{8,12},{12,16},{16,20},{20,24},{24,28},{1,5},{5,9},{9,... | collective-permute-start | bytes 1474568 | tf_op jit(solution)/shard_map/ppermute | solution.py:35
  6.5 1.9 collective-permute-start.1
  8.5 0.1 reshape.143
  8.6 0.1 reshape.155
  8.7 4.8 %gather_fusion.3 = f32[736]{0:T(1024)S(1)} fusion(f32[31]{0:T(128)S(1)} %copy-done.1, s32[1024]{0:T(1024)S(1)} %get-tuple-element.47), kind=kCustom, calls=%fused_computation.2.clone | custom fusion | bytes 8832 | tf_op jit(solution)/shard_map/jit(_take)/gather | solution.py:52
  13.5 0.1 reshape.158
  13.8 0.7 fusion.577
  14.5 0.7 fusion.576
  15.2 4.7 %collective-permute-done.1 = f32[16,15,512]{2,1,0:T(8,128)S(1)} collective-permute-done((f32[16,15,512]{2,1,0:T(8,128)S(1)}, f32[16,15,512]{2,1,0:T(8,128)S(1)}, u32[]{:S(2)}, u32[]{:S(2)}) %collective-permute-start.1) | collective-permute-done | bytes 491552 | tf_op jit(solution)/shard_map/ppermute | solution.py:36
  19.9 1.0 fusion.15
  20.9 23.0 %fusion.23 = f32[16,16,512]{2,1,0:T(8,128)S(1)} fusion(f32[16,16,512]{2,1,0:T(8,128)S(1)} %fusion.15, f32[]{:T(128)} %bitcast.35, f32[]{:T(128)} %bitcast.34, f32[]{:T(128)} %bitcast.33, f32[]{:T(128)} %bitcast.32, f32[]{:T(128)} %bitcast.31, f32[]{:T(128)} %bitcast.30, f32[]{:T(128)} %bitcast.29, f32[]{:T(128)} %bitcast.28, f32[]{:T(128)} %bitcast.27, ...), kind=kOutput, calls=%fused_computation.27 | convolution fusion | flops 824705024 | bytes 1048700 | tf_op jit(solution)/shard_map/dot_general | solution.py:78
  43.9 0.1 fusion.223
  44.1 3.4 %collective-permute-start.2 = (f32[16,16,128]{2,1,0:T(8,128)S(1)}, f32[16,16,128]{2,1,0:T(8,128)S(1)}, u32[]{:S(2)}, u32[]{:S(2)}) collective-permute-start(f32[16,16,128]{2,1,0:T(8,128)S(1)} %get-tuple-element.9), channel_id=1, source_target_pairs={{0,3},{1,0},{2,1},{3,2},{4,7},{5,4},{6,5},{7,6},{8,11},{9,8},{10,9... | collective-permute-start | bytes 393224 | tf_op jit(solution)/shard_map/ppermute | solution.py:19
  47.5 24.7 %gather_fusion.2 = f32[4096]{0:T(1024)S(1)} fusion(f32[31]{0:T(128)S(1)} %copy-done, s32[4096]{0:T(1024)S(1)} %get-tuple-element.45), kind=kCustom, calls=%fused_computation.3.clone | custom fusion | bytes 49152 | tf_op jit(solution)/shard_map/jit(_take)/gather | solution.py:52
  72.3 0.4 collective-permute-start.4
  72.8 5.1 %collective-permute-done.4 = f32[16,16,128]{2,1,0:T(8,128)S(1)} collective-permute-done((f32[16,16,128]{2,1,0:T(8,128)S(1)}, f32[16,16,128]{2,1,0:T(8,128)S(1)}, u32[]{:S(2)}, u32[]{:S(2)}) %collective-permute-start.4) | collective-permute-done | bytes 131104 | tf_op jit(solution)/shard_map/ppermute | solution.py:19
  78.1 0.7 fusion.226
  78.8 1.1 copy.21
  79.9 3.5 %all-to-all-start = ((f32[64,16,128]{2,1,0:T(8,128)}), f32[64,16,128]{2,1,0:T(8,128)S(1)}, u32[]{:S(2)}, u32[]{:S(2)}) async-start(f32[64,16,128]{2,1,0:T(8,128)} %copy.21), calls=%async_computation | async-start | bytes 1048576 | tf_op jit(solution)/shard_map/all_to_all | solution.py:96
  83.4 3.7 %copy.23 = f32[16,16,512]{1,0,2:T(8,128)} copy(f32[16,16,512]{2,1,0:T(8,128)S(1)} %copy-done.3) | data formatting | bytes 1048576 | tf_op args[1]
  87.1 6.4 %all-to-all-done = f32[64,16,128]{2,1,0:T(8,128)S(1)} async-done(((f32[64,16,128]{2,1,0:T(8,128)}), f32[64,16,128]{2,1,0:T(8,128)S(1)}, u32[]{:S(2)}, u32[]{:S(2)}) %all-to-all-start) | async-done | bytes 524320 | tf_op jit(solution)/shard_map/all_to_all | solution.py:96
  93.5 2.8 %copy.22 = f32[16,16,4,128]{1,0,3,2:T(8,128)} copy(f32[16,16,4,128]{3,1,0,2:T(8,128)S(1)} %bitcast.115) | data formatting | bytes 1048576 | tf_op jit(solution)/shard_map/all_to_all | solution.py:96
  96.3 6.0 %bitcast_divide_fusion = f32[16,16,512]{1,0,2:T(8,128)} fusion(f32[16,16,512]{1,0,2:T(8,128)} %copy.23, f32[16,16,4,128]{1,0,3,2:T(8,128)} %copy.22), kind=kLoop, calls=%fused_computation.4 | loop fusion | flops 131072 | bytes 1572864 | tf_op jit(solution)/shard_map/div | solution.py:97
  102.3 4.6 %reshape.229 = f32[4,1,32768]{2,1,0:T(1,128)} reshape(f32[512,16,16]{2,1,0:T(8,128)} %bitcast.113) | data formatting | bytes 1048576
  106.9 3.7 %all-to-all-start.1 = ((f32[4,1,32768]{2,1,0:T(1,128)}), f32[4,1,32768]{2,1,0:T(1,128)S(1)}, u32[]{:S(2)}, u32[]{:S(2)}) async-start(f32[4,1,32768]{2,1,0:T(1,128)} %reshape.229), calls=%async_computation.1 | async-start | bytes 1048576 | tf_op jit(solution)/shard_map/all_to_all | solution.py:99
  110.6 24.7 %gather_fusion.1 = f32[4096]{0:T(1024)S(1)} fusion(f32[31]{0:T(128)S(1)} %copy-done, s32[4096]{0:T(1024)S(1)} %get-tuple-element.46), kind=kCustom, calls=%fused_computation.1.clone | custom fusion | bytes 49152 | tf_op jit(solution)/shard_map/jit(_take)/gather | solution.py:52
  135.4 0.5 broadcast.950
  135.9 2.2 reduce
  138.1 3.4 %reshape.230 = f32[512,16,16]{2,1,0:T(8,128)} reshape(f32[4,32768]{1,0:T(4,128)S(1)} %reduce) | data formatting | bytes 1048576
  141.5 3.3 %copy.24 = f32[16,16,4,128]{3,0,2,1:T(8,128)S(1)} copy(f32[16,16,4,128]{1,0,3,2:T(8,128)} %bitcast.114) | data formatting | bytes 1048576 | tf_op jit(solution)/shard_map/all_to_all | solution.py:99
  144.8 0.6 fusion.383
  145.5 0.3 copy.26
  145.8 18.0 %all_to_all.54 = f32[64,16,128]{2,1,0:T(8,128)S(1)} all-to-all(f32[64,16,128]{2,1,0:T(8,128)S(1)} %copy.26), channel_id=1, replica_groups=mesh['tile'=8,'slab'=4] {'slab'}, dimensions={0} | all-to-all | bytes 1048576 | tf_op jit(solution)/shard_map/all_to_all | solution.py:101
  163.7 0.3 copy.40
  164.1 0.2 all_to_all.50
  164.3 23.0 %fusion.21 = f32[16,16,512]{2,1,0:T(8,128)S(1)} fusion(f32[16,16,512]{2,1,0:T(8,128)S(1)} %all_to_all.50, f32[]{:T(128)} %bitcast.35, f32[]{:T(128)} %bitcast.34, f32[]{:T(128)} %bitcast.33, f32[]{:T(128)} %bitcast.32, f32[]{:T(128)} %bitcast.31, f32[]{:T(128)} %bitcast.30, f32[]{:T(128)} %bitcast.29, f32[]{:T(128)} %bitcast.28, f32[]{:T(128)} %bitcast.27, ...), kind=kOutput, calls=%fused_computation.25 | convolution fusion | flops 824967168 | bytes 1048700 | tf_op jit(solution)/shard_map/dot_general | solution.py:78
  187.3 0.1 fusion.572
  187.4 9.8 %collective-permute-start.5 = (f32[16,15,512]{2,1,0:T(8,128)S(1)}, f32[16,15,512]{2,1,0:T(8,128)S(1)}, u32[]{:S(2)}, u32[]{:S(2)}) collective-permute-start(f32[16,15,512]{2,1,0:T(8,128)S(1)} %get-tuple-element.4), channel_id=1, source_target_pairs={{0,4},{4,8},{8,12},{12,16},{16,20},{20,24},{24,28},{1,5},{5,9},{9,... | collective-permute-start | bytes 1474568 | tf_op jit(solution)/shard_map/ppermute | solution.py:35
  197.1 1.9 collective-permute-start.6
  199.1 4.8 %gather_fusion = f32[736]{0:T(1024)S(1)} fusion(f32[31]{0:T(128)S(1)} %copy-done.1, s32[1024]{0:T(1024)S(1)} %get-tuple-element.48), kind=kCustom, calls=%fused_computation.clone | custom fusion | bytes 8832 | tf_op jit(solution)/shard_map/jit(_take)/gather | solution.py:52
  204.0 3.7 %collective-permute-done.6 = f32[16,15,512]{2,1,0:T(8,128)S(1)} collective-permute-done((f32[16,15,512]{2,1,0:T(8,128)S(1)}, f32[16,15,512]{2,1,0:T(8,128)S(1)}, u32[]{:S(2)}, u32[]{:S(2)}) %collective-permute-start.6) | collective-permute-done | bytes 491552 | tf_op jit(solution)/shard_map/ppermute | solution.py:36
  207.6 1.0 fusion.18
  208.7 0.7 fusion.224
  209.4 1.9 collective-permute-start.7
  211.4 2.4 %collective-permute-start.8 = (f32[16,1,256]{2,1,0:T(1,128)S(1)}, f32[16,1,256]{2,1,0:T(1,128)S(1)}, u32[]{:S(2)}, u32[]{:S(2)}) collective-permute-start(f32[16,1,256]{2,1,0:T(1,128)S(1)} %get-tuple-element.13), channel_id=1, source_target_pairs={{4,0},{8,4},{12,8},{16,12},{20,16},{24,20},{28,24},{5,1},{9,5},{13... | collective-permute-start | bytes 49160 | tf_op jit(solution)/shard_map/ppermute | solution.py:36
  213.8 2.6 %collective-permute-done.8 = f32[16,1,256]{2,1,0:T(1,128)S(1)} collective-permute-done((f32[16,1,256]{2,1,0:T(1,128)S(1)}, f32[16,1,256]{2,1,0:T(1,128)S(1)}, u32[]{:S(2)}, u32[]{:S(2)}) %collective-permute-start.8) | collective-permute-done | bytes 16416 | tf_op jit(solution)/shard_map/ppermute | solution.py:36
  216.4 1.0 convolution_bitcast_fusion
  (43 shorter events, 0.7 us)
Async XLA Ops:
  0.6 46.9 %copy-start = (f32[31]{0:T(128)S(1)}, f32[31]{0:T(128)}, u32[]{:S(2)}) copy-start(f32[31]{0:T(128)} %param.15) | copy-start | bytes 376
  0.6 8.0 %copy-start.1 = (f32[31]{0:T(128)S(1)}, f32[31]{0:T(128)}, u32[]{:S(2)}) copy-start(f32[31]{0:T(128)} %param.13) | copy-start | bytes 376
  2.0 13.2 %collective-permute-start = (f32[16,15,512]{2,1,0:T(8,128)S(1)}, f32[16,15,512]{2,1,0:T(8,128)S(1)}, u32[]{:S(2)}, u32[]{:S(2)}) collective-permute-start(f32[16,15,512]{2,1,0:T(8,128)S(1)} %get-tuple-element.10), channel_id=1, source_target_pairs={{0,4},{4,8},{8,12},{12,16},{16,20},{20,24},{24,28},{1,5},{5,9},{9,... | collective-permute-start | bytes 1474568 | tf_op jit(solution)/shard_map/ppermute | solution.py:35
  6.5 13.4 %collective-permute-start.1 = (f32[16,15,512]{2,1,0:T(8,128)S(1)}, f32[16,15,512]{2,1,0:T(8,128)S(1)}, u32[]{:S(2)}, u32[]{:S(2)}) collective-permute-start(f32[16,15,512]{2,1,0:T(8,128)S(1)} %get-tuple-element.11), channel_id=1, source_target_pairs={{4,0},{8,4},{12,8},{16,12},{20,16},{24,20},{28,24},{5,1},{9,5},{13... | collective-permute-start | bytes 1474568 | tf_op jit(solution)/shard_map/ppermute | solution.py:36
  8.7 5.1 %copy-start.5 = (f32[31]{0:T(128)S(1)}, f32[31]{0:T(128)}, u32[]{:S(2)}) copy-start(f32[31]{0:T(128)} %param.14) | copy-start | bytes 376
  8.7 11.2 %copy-start.2 = (f32[16,16,512]{2,1,0:T(8,128)S(1)}, f32[16,16,512]{2,1,0:T(8,128)}, u32[]{:S(2)}) copy-start(f32[16,16,512]{2,1,0:T(8,128)} %param.11) | copy-start | bytes 1572868
  44.1 28.6 %collective-permute-start.2 = (f32[16,16,128]{2,1,0:T(8,128)S(1)}, f32[16,16,128]{2,1,0:T(8,128)S(1)}, u32[]{:S(2)}, u32[]{:S(2)}) collective-permute-start(f32[16,16,128]{2,1,0:T(8,128)S(1)} %get-tuple-element.9), channel_id=1, source_target_pairs={{0,3},{1,0},{2,1},{3,2},{4,7},{5,4},{6,5},{7,6},{8,11},{9,8},{10,9... | collective-permute-start | bytes 393224 | tf_op jit(solution)/shard_map/ppermute | solution.py:19
  47.5 25.3 %collective-permute-start.3 = (f32[16,16,128]{2,1,0:T(8,128)S(1)}, f32[16,16,128]{2,1,0:T(8,128)S(1)}, u32[]{:S(2)}, u32[]{:S(2)}) collective-permute-start(f32[16,16,128]{2,1,0:T(8,128)S(1)} %get-tuple-element.8), channel_id=1, source_target_pairs={{0,2},{1,3},{2,0},{3,1},{4,6},{5,7},{6,4},{7,5},{8,10},{9,11},{10,... | collective-permute-start | bytes 393224 | tf_op jit(solution)/shard_map/ppermute | solution.py:19
  72.3 5.6 %collective-permute-start.4 = (f32[16,16,128]{2,1,0:T(8,128)S(1)}, f32[16,16,128]{2,1,0:T(8,128)S(1)}, u32[]{:S(2)}, u32[]{:S(2)}) collective-permute-start(f32[16,16,128]{2,1,0:T(8,128)S(1)} %get-tuple-element.7), channel_id=1, source_target_pairs={{0,1},{1,2},{2,3},{3,0},{4,5},{5,6},{6,7},{7,4},{8,9},{9,10},{10,1... | collective-permute-start | bytes 393224 | tf_op jit(solution)/shard_map/ppermute | solution.py:19
  78.1 5.3 %copy-start.3 = (f32[16,16,512]{2,1,0:T(8,128)S(1)}, f32[16,16,512]{2,1,0:T(8,128)}, u32[]{:S(2)}) copy-start(f32[16,16,512]{2,1,0:T(8,128)} %param.12) | copy-start | bytes 1572868
  79.9 13.6 %all-to-all-start = ((f32[64,16,128]{2,1,0:T(8,128)}), f32[64,16,128]{2,1,0:T(8,128)S(1)}, u32[]{:S(2)}, u32[]{:S(2)}) async-start(f32[64,16,128]{2,1,0:T(8,128)} %copy.21), calls=%async_computation | async-start | bytes 1048576 | tf_op jit(solution)/shard_map/all_to_all | solution.py:96
  106.9 28.4 %all-to-all-start.1 = ((f32[4,1,32768]{2,1,0:T(1,128)}), f32[4,1,32768]{2,1,0:T(1,128)S(1)}, u32[]{:S(2)}, u32[]{:S(2)}) async-start(f32[4,1,32768]{2,1,0:T(1,128)} %reshape.229), calls=%async_computation.1 | async-start | bytes 1048576 | tf_op jit(solution)/shard_map/all_to_all | solution.py:99
  187.4 16.6 %collective-permute-start.5 = (f32[16,15,512]{2,1,0:T(8,128)S(1)}, f32[16,15,512]{2,1,0:T(8,128)S(1)}, u32[]{:S(2)}, u32[]{:S(2)}) collective-permute-start(f32[16,15,512]{2,1,0:T(8,128)S(1)} %get-tuple-element.4), channel_id=1, source_target_pairs={{0,4},{4,8},{8,12},{12,16},{16,20},{20,24},{24,28},{1,5},{5,9},{9,... | collective-permute-start | bytes 1474568 | tf_op jit(solution)/shard_map/ppermute | solution.py:35
  197.1 10.5 %collective-permute-start.6 = (f32[16,15,512]{2,1,0:T(8,128)S(1)}, f32[16,15,512]{2,1,0:T(8,128)S(1)}, u32[]{:S(2)}, u32[]{:S(2)}) collective-permute-start(f32[16,15,512]{2,1,0:T(8,128)S(1)} %get-tuple-element.6), channel_id=1, source_target_pairs={{4,0},{8,4},{12,8},{16,12},{20,16},{24,20},{28,24},{5,1},{9,5},{13... | collective-permute-start | bytes 1474568 | tf_op jit(solution)/shard_map/ppermute | solution.py:36
  208.7 8.8 %copy-start.4 = (f32[16,16,512]{2,1,0:T(8,128)}, f32[16,16,512]{2,1,0:T(8,128)S(1)}, u32[]{:S(2)}) copy-start(f32[16,16,512]{2,1,0:T(8,128)S(1)} %fusion.18) | copy-start | bytes 1572868
  209.4 4.4 %collective-permute-start.7 = (f32[16,1,256]{2,1,0:T(1,128)S(1)}, f32[16,1,256]{2,1,0:T(1,128)S(1)}, u32[]{:S(2)}, u32[]{:S(2)}) collective-permute-start(f32[16,1,256]{2,1,0:T(1,128)S(1)} %get-tuple-element.12), channel_id=1, source_target_pairs={{0,4},{4,8},{8,12},{12,16},{16,20},{20,24},{24,28},{1,5},{5,9},{9,... | collective-permute-start | bytes 49160 | tf_op jit(solution)/shard_map/ppermute | solution.py:35
  211.4 5.1 %collective-permute-start.8 = (f32[16,1,256]{2,1,0:T(1,128)S(1)}, f32[16,1,256]{2,1,0:T(1,128)S(1)}, u32[]{:S(2)}, u32[]{:S(2)}) collective-permute-start(f32[16,1,256]{2,1,0:T(1,128)S(1)} %get-tuple-element.13), channel_id=1, source_target_pairs={{4,0},{8,4},{12,8},{16,12},{20,16},{24,20},{28,24},{5,1},{9,5},{13... | collective-permute-start | bytes 49160 | tf_op jit(solution)/shard_map/ppermute | solution.py:36
